TPU v7x, 128 devices: a whole 4x4x4 slice. The times are simulated.
128 devices in a mesh: xb: 16 (over y, z), yb: 8 (over x, core).
Axes of the slice: x: 4, y: 4, z: 4, core: 2. Of those that a mesh axis runs over, the one named last changes fastest.
Arguments:
- initial_guess: float32 [128, 512, 256], P('xb', 'yb'), may hold values from -4 to 4
- right_side: float32 [128, 512, 256], P('xb', 'yb'), may hold values from -8 to 8
- coefficient: float32 [128, 512, 256], P('xb', 'yb'), may hold values from 0.3 to 3
Outputs:
- fine_field: float32 [128, 512, 256], P('xb', 'yb')
- middle_field: float32 [64, 256, 128], P('xb', 'yb')
- lower_field: float32 [32, 128, 64], P('xb', 'yb')
- coarse_field: float32 [16, 64, 32], P('xb', 'yb')
All inputs are finite; a program needn't handle non-finite values.
Results may differ from a plain program's by a relative error of at most 0.00002.
Values sent between devices are 32-bit elements; how exact they have to be, the bound alone decides.
No kernel may reach another device: no remote copies, remote signals or barrier semaphores. Data moves between devices by JAX's collectives and lax.ppermute only.
A program may use at most 192 MiB of HBM per device.

v0:
```python
import jax
import jax.numpy as jnp
from jax import lax
from jax.sharding import PartitionSpec as P

COARSE_ITERS = 8
damping_alpha = 0.05
cheb_theta = 1.15
cheb_delta = 0.85
cheb_sigma = cheb_theta / cheb_delta
cheb_first = 1.0 / cheb_sigma
cheb_second = 1.0 / (2.0 * cheb_sigma - cheb_first)
cheb_carry = cheb_second * cheb_first
cheb_resid = 2.0 * cheb_second / cheb_delta
jacobi_weight = 0.8


def with_halo(block, sides, width):
    for axis, dim in sides:
        count = lax.axis_size(axis)
        forward = [(i, i + 1) for i in range(count - 1)]
        backward = [(target, source) for source, target in forward]
        low = lax.ppermute(
            lax.slice_in_dim(block, block.shape[dim] - width, None, axis=dim), axis, forward
        )
        high = lax.ppermute(lax.slice_in_dim(block, 0, width, axis=dim), axis, backward)
        block = jnp.concatenate([low, block, high], axis=dim)
    return block


def neighbours(padded):
    return [
        padded[2:, 1:-1, 1:-1],
        padded[:-2, 1:-1, 1:-1],
        padded[1:-1, 2:, 1:-1],
        padded[1:-1, :-2, 1:-1],
        padded[1:-1, 1:-1, 2:],
        padded[1:-1, 1:-1, :-2],
    ]


def face_weights(padded_coef, scale):
    centre = padded_coef[1:-1, 1:-1, 1:-1]
    weights = [0.5 * scale * (centre + other) for other in neighbours(padded_coef)]
    diagonal = damping_alpha + weights[0]
    for other in weights[1:]:
        diagonal = diagonal + other
    return (weights, diagonal)


def apply_operator(padded, field, weights, diagonal):
    result = diagonal * field
    for weight, other in zip(weights, neighbours(padded)):
        result = result - weight * other
    return result


def smooth_level(start, right_side, coefficient, scale, extend, padded_coef=None):
    padded_coef = extend(coefficient)
    weights, diagonal = face_weights(padded_coef, scale)
    if start is None:
        start = jnp.zeros_like(right_side)
        residual = right_side
    else:
        residual = right_side - apply_operator(extend(start), start, weights, diagonal)
    first_step = residual / (cheb_theta * diagonal)
    first = start + first_step
    residual = right_side - apply_operator(extend(first), first, weights, diagonal)
    second_step = cheb_carry * first_step + cheb_resid * residual / diagonal
    second = first + second_step
    residual = right_side - apply_operator(extend(second), second, weights, diagonal)
    return (second, residual)


def pair_matrix(count):
    rows = jnp.arange(count // 2)[:, None]
    cols = jnp.arange(count)[None, :] // 2
    return (rows == cols).astype(jnp.float32)


def restrict_field(field):
    sx, sy, sz = field.shape
    halves = field.reshape(sx // 2, 2, sy, sz)
    summed = halves[:, 0] + halves[:, 1]
    summed = jnp.einsum("xyZ,zZ->xyz", summed, pair_matrix(sz), precision=lax.Precision.HIGHEST)
    pairs_y = jnp.broadcast_to(pair_matrix(sy), (sx // 2, sy // 2, sy))
    summed = jnp.einsum("xyY,xYz->xyz", pairs_y, summed, precision=lax.Precision.HIGHEST)
    return summed * 0.125


def coarse_solve(right_side, coefficient, scale, extend):
    weights, diagonal = face_weights(extend(coefficient), scale)
    field = jnp.zeros_like(right_side)
    for repeat in range(COARSE_ITERS):
        field = (
            field
            + jacobi_weight
            * (right_side - apply_operator(extend(field), field, weights, diagonal))
            / diagonal
        )
    leftover = right_side - apply_operator(extend(field), field, weights, diagonal)
    ones_field = jnp.ones_like(right_side)
    image_ones = apply_operator(extend(ones_field), ones_field, weights, diagonal)
    return field + jnp.sum(leftover) / jnp.sum(image_ones)


def extend_all(field):
    return jnp.pad(field, 1)


def extend_local(field):
    padded = with_halo(field, (("xb", 0), ("yb", 1)), 1)
    return jnp.pad(padded, ((0, 0), (0, 0), (1, 1)))


def collect_grid(right_side, coefficient):
    sx, sy, sz = right_side.shape
    count_x = lax.axis_size("xb")
    count_y = lax.axis_size("yb")
    flat = (
        lax.all_gather(right_side.reshape(1, -1), ("xb", "yb"), axis=0, tiled=True),
        lax.all_gather(coefficient.reshape(1, -1), ("xb", "yb"), axis=0, tiled=True),
    )
    return tuple(
        (
            piece.reshape(count_x, count_y, sx, sy, sz)
            .transpose(0, 2, 1, 3, 4)
            .reshape(count_x * sx, count_y * sy, sz)
            for piece in flat
        )
    )


def own_block(whole, shape):
    start_x = lax.axis_index("xb") * shape[0]
    start_y = lax.axis_index("yb") * shape[1]
    return lax.dynamic_slice(whole, (start_x, start_y, jnp.int32(0)), shape)


def per_device(initial_guess, right_side, coefficient):
    fine, fine_res = smooth_level(initial_guess, right_side, coefficient, 1.0, extend_local, None)
    mid_coef = restrict_field(coefficient)
    middle, mid_res = smooth_level(
        None, restrict_field(fine_res), mid_coef, 0.25, extend_local, None
    )
    low_coef = restrict_field(mid_coef)
    low_rhs = restrict_field(mid_res)
    lower, low_res = smooth_level(None, low_rhs, low_coef, 0.0625, extend_local, None)
    coarse_rhs, coarse_coef = collect_grid(restrict_field(low_res), restrict_field(low_coef))
    coarse_whole = coarse_solve(coarse_rhs, coarse_coef, 0.015625, extend_all)
    sx, sy, sz = right_side.shape
    coarse = own_block(coarse_whole, (sx // 8, sy // 8, sz // 8))
    return (fine, middle, lower, coarse)


def solution(mesh):
    placed = (P("xb", "yb", None), P("xb", "yb", None), P("xb", "yb", None))
    return jax.shard_map(
        per_device,
        mesh=mesh,
        in_specs=placed,
        out_specs=(
            P("xb", "yb", None),
            P("xb", "yb", None),
            P("xb", "yb", None),
            P("xb", "yb", None),
        ),
        check_vma=False,
    )
```

profile of v0, /device:TPU:1, one launch (start us, length us, event | category | flops | bytes accessed | tf_op | source)
XLA Modules:
  0.0 239.6 jit_solution(1692704037954307134)
XLA Ops:
  0.6 0.9 fusion.348
  1.6 4.4 %collective-permute-start.1 = (f32[1,64,256]{2,1,0:T(8,128)S(1)}, f32[1,64,256]{2,1,0:T(8,128)S(1)}, u32[]{:S(2)}, u32[]{:S(2)}) collective-permute-start(f32[1,64,256]{2,1,0:T(8,128)S(1)} %get-tuple-element.31), channel_id=1, source_target_pairs={{0,8},{8,16},{16,24},{24,32},{32,40},{40,48},{48,56},{56,64},{64,7... | collective-permute-start | bytes 196616 | tf_op jit(solution)/shard_map/ppermute | solution.py:23
  6.0 1.3 collective-permute-start
  7.3 0.9 fusion.349
  8.1 4.2 %collective-permute-start.5 = (f32[1,64,256]{2,1,0:T(8,128)S(1)}, f32[1,64,256]{2,1,0:T(8,128)S(1)}, u32[]{:S(2)}, u32[]{:S(2)}) collective-permute-start(f32[1,64,256]{2,1,0:T(8,128)S(1)} %get-tuple-element.33), channel_id=1, source_target_pairs={{0,8},{8,16},{16,24},{24,32},{32,40},{40,48},{48,56},{56,64},{64,7... | collective-permute-start | bytes 196616 | tf_op jit(solution)/shard_map/ppermute | solution.py:23
  12.3 1.3 collective-permute-start.4
  13.7 1.4 fusion.217
  15.3 1.3 collective-permute-start.16
  16.8 4.6 %collective-permute-start.17 = (f32[1,32,128]{2,1,0:T(8,128)S(1)}, f32[1,32,128]{2,1,0:T(8,128)S(1)}, u32[]{:S(2)}, u32[]{:S(2)}) collective-permute-start(f32[1,32,128]{2,1,0:T(8,128)S(1)} %get-tuple-element.44), channel_id=1, source_target_pairs={{0,8},{8,16},{16,24},{24,32},{32,40},{40,48},{48,56},{56,64},{64,7... | collective-permute-start | bytes 49160 | tf_op jit(solution)/shard_map/ppermute | solution.py:23
  21.5 3.8 %collective-permute-start.2 = (f32[10,1,256]{2,1,0:T(1,128)S(1)}, f32[10,1,256]{2,1,0:T(1,128)S(1)}, u32[]{:S(2)}, u32[]{:S(2)}) collective-permute-start(f32[10,1,256]{2,1,0:T(1,128)S(1)} %get-tuple-element.23), channel_id=1, source_target_pairs={{1,0},{2,1},{3,2},{4,3},{5,4},{6,5},{7,6},{9,8},{10,9},{11,10},{12... | collective-permute-start | bytes 30728 | tf_op jit(solution)/shard_map/ppermute | solution.py:26
  25.4 3.0 %collective-permute-start.3 = (f32[10,1,256]{2,1,0:T(1,128)S(1)}, f32[10,1,256]{2,1,0:T(1,128)S(1)}, u32[]{:S(2)}, u32[]{:S(2)}) collective-permute-start(f32[10,1,256]{2,1,0:T(1,128)S(1)} %get-tuple-element.22), channel_id=1, source_target_pairs={{0,1},{1,2},{2,3},{3,4},{4,5},{5,6},{6,7},{8,9},{9,10},{10,11},{11... | collective-permute-start | bytes 30728 | tf_op jit(solution)/shard_map/ppermute | solution.py:23
  28.5 1.9 collective-permute-start.6
  30.4 3.6 %collective-permute-start.7 = (f32[10,1,256]{2,1,0:T(1,128)S(1)}, f32[10,1,256]{2,1,0:T(1,128)S(1)}, u32[]{:S(2)}, u32[]{:S(2)}) collective-permute-start(f32[10,1,256]{2,1,0:T(1,128)S(1)} %get-tuple-element.24), channel_id=1, source_target_pairs={{0,1},{1,2},{2,3},{3,4},{4,5},{5,6},{6,7},{8,9},{9,10},{10,11},{11... | collective-permute-start | bytes 30728 | tf_op jit(solution)/shard_map/ppermute | solution.py:23
  35.6 1.2 fusion.342
  36.8 1.3 collective-permute-start.8
  38.1 4.3 %collective-permute-start.9 = (f32[1,64,256]{2,1,0:T(8,128)S(1)}, f32[1,64,256]{2,1,0:T(8,128)S(1)}, u32[]{:S(2)}, u32[]{:S(2)}) collective-permute-start(f32[1,64,256]{2,1,0:T(8,128)S(1)} %get-tuple-element.28), channel_id=1, source_target_pairs={{0,8},{8,16},{16,24},{24,32},{32,40},{40,48},{48,56},{56,64},{64,7... | collective-permute-start | bytes 196616 | tf_op jit(solution)/shard_map/ppermute | solution.py:23
  42.4 1.3 collective-permute-done.9
  43.7 1.9 collective-permute-start.10
  45.7 4.8 %collective-permute-start.11 = (f32[10,1,256]{2,1,0:T(1,128)S(1)}, f32[10,1,256]{2,1,0:T(1,128)S(1)}, u32[]{:S(2)}, u32[]{:S(2)}) collective-permute-start(f32[10,1,256]{2,1,0:T(1,128)S(1)} %get-tuple-element.20), channel_id=1, source_target_pairs={{0,1},{1,2},{2,3},{3,4},{4,5},{5,6},{6,7},{8,9},{9,10},{10,11},{11... | collective-permute-start | bytes 30728 | tf_op jit(solution)/shard_map/ppermute | solution.py:23
  50.6 0.6 collective-permute-done.11
  51.7 1.2 fusion.181
  53.0 1.3 collective-permute-start.12
  54.3 4.6 %collective-permute-start.13 = (f32[1,64,256]{2,1,0:T(8,128)S(1)}, f32[1,64,256]{2,1,0:T(8,128)S(1)}, u32[]{:S(2)}, u32[]{:S(2)}) collective-permute-start(f32[1,64,256]{2,1,0:T(8,128)S(1)} %get-tuple-element.26), channel_id=1, source_target_pairs={{0,8},{8,16},{16,24},{24,32},{32,40},{40,48},{48,56},{56,64},{64,7... | collective-permute-start | bytes 196616 | tf_op jit(solution)/shard_map/ppermute | solution.py:23
  58.9 1.9 collective-permute-start.18
  60.9 4.5 %collective-permute-start.19 = (f32[6,1,128]{2,1,0:T(1,128)S(1)}, f32[6,1,128]{2,1,0:T(1,128)S(1)}, u32[]{:S(2)}, u32[]{:S(2)}) collective-permute-start(f32[6,1,128]{2,1,0:T(1,128)S(1)} %get-tuple-element.38), channel_id=1, source_target_pairs={{0,1},{1,2},{2,3},{3,4},{4,5},{5,6},{6,7},{8,9},{9,10},{10,11},{11... | collective-permute-start | bytes 9224 | tf_op jit(solution)/shard_map/ppermute | solution.py:23
  65.4 1.9 collective-permute-start.14
  67.3 3.6 %collective-permute-start.15 = (f32[10,1,256]{2,1,0:T(1,128)S(1)}, f32[10,1,256]{2,1,0:T(1,128)S(1)}, u32[]{:S(2)}, u32[]{:S(2)}) collective-permute-start(f32[10,1,256]{2,1,0:T(1,128)S(1)} %get-tuple-element.18), channel_id=1, source_target_pairs={{0,1},{1,2},{2,3},{3,4},{4,5},{5,6},{6,7},{8,9},{9,10},{10,11},{11... | collective-permute-start | bytes 30728 | tf_op jit(solution)/shard_map/ppermute | solution.py:23
  72.2 1.1 fusion.166
  73.9 1.3 collective-permute-start.20
  75.2 5.8 %collective-permute-start.21 = (f32[1,32,128]{2,1,0:T(8,128)S(1)}, f32[1,32,128]{2,1,0:T(8,128)S(1)}, u32[]{:S(2)}, u32[]{:S(2)}) collective-permute-start(f32[1,32,128]{2,1,0:T(8,128)S(1)} %get-tuple-element.42), channel_id=1, source_target_pairs={{0,8},{8,16},{16,24},{24,32},{32,40},{40,48},{48,56},{56,64},{64,7... | collective-permute-start | bytes 49160 | tf_op jit(solution)/shard_map/ppermute | solution.py:23
  81.1 1.3 collective-permute-start.28
  82.4 6.4 %collective-permute-start.29 = (f32[1,16,64]{2,1,0:T(8,128)S(1)}, f32[1,16,64]{2,1,0:T(8,128)S(1)}, u32[]{:S(2)}, u32[]{:S(2)}) collective-permute-start(f32[1,16,64]{2,1,0:T(8,128)S(1)} %get-tuple-element.56), channel_id=1, source_target_pairs={{0,8},{8,16},{16,24},{24,32},{32,40},{40,48},{48,56},{56,64},{64,7... | collective-permute-start | bytes 12296 | tf_op jit(solution)/shard_map/ppermute | solution.py:23
  88.8 1.9 collective-permute-start.22
  90.7 4.8 %collective-permute-start.23 = (f32[6,1,128]{2,1,0:T(1,128)S(1)}, f32[6,1,128]{2,1,0:T(1,128)S(1)}, u32[]{:S(2)}, u32[]{:S(2)}) collective-permute-start(f32[6,1,128]{2,1,0:T(1,128)S(1)} %get-tuple-element.36), channel_id=1, source_target_pairs={{0,1},{1,2},{2,3},{3,4},{4,5},{5,6},{6,7},{8,9},{9,10},{10,11},{11... | collective-permute-start | bytes 9224 | tf_op jit(solution)/shard_map/ppermute | solution.py:23
  95.6 0.6 collective-permute-done.23
  96.6 1.3 collective-permute-start.24
  97.9 6.7 %collective-permute-start.25 = (f32[1,32,128]{2,1,0:T(8,128)S(1)}, f32[1,32,128]{2,1,0:T(8,128)S(1)}, u32[]{:S(2)}, u32[]{:S(2)}) collective-permute-start(f32[1,32,128]{2,1,0:T(8,128)S(1)} %get-tuple-element.40), channel_id=1, source_target_pairs={{0,8},{8,16},{16,24},{24,32},{32,40},{40,48},{48,56},{56,64},{64,7... | collective-permute-start | bytes 49160 | tf_op jit(solution)/shard_map/ppermute | solution.py:23
  104.6 1.9 collective-permute-start.30
  106.6 4.5 %collective-permute-start.31 = (f32[4,1,64]{2,1,0:T(1,128)S(1)}, f32[4,1,64]{2,1,0:T(1,128)S(1)}, u32[]{:S(2)}, u32[]{:S(2)}) collective-permute-start(f32[4,1,64]{2,1,0:T(1,128)S(1)} %get-tuple-element.50), channel_id=1, source_target_pairs={{0,1},{1,2},{2,3},{3,4},{4,5},{5,6},{6,7},{8,9},{9,10},{10,11},{11... | collective-permute-start | bytes 3080 | tf_op jit(solution)/shard_map/ppermute | solution.py:23
  111.1 1.9 collective-permute-start.26
  113.0 3.6 %collective-permute-start.27 = (f32[6,1,128]{2,1,0:T(1,128)S(1)}, f32[6,1,128]{2,1,0:T(1,128)S(1)}, u32[]{:S(2)}, u32[]{:S(2)}) collective-permute-start(f32[6,1,128]{2,1,0:T(1,128)S(1)} %get-tuple-element.34), channel_id=1, source_target_pairs={{0,1},{1,2},{2,3},{3,4},{4,5},{5,6},{6,7},{8,9},{9,10},{10,11},{11... | collective-permute-start | bytes 9224 | tf_op jit(solution)/shard_map/ppermute | solution.py:23
  116.8 0.6 collective-permute-done.27
  118.0 1.3 collective-permute-start.32
  119.3 6.4 %collective-permute-start.33 = (f32[1,16,64]{2,1,0:T(8,128)S(1)}, f32[1,16,64]{2,1,0:T(8,128)S(1)}, u32[]{:S(2)}, u32[]{:S(2)}) collective-permute-start(f32[1,16,64]{2,1,0:T(8,128)S(1)} %get-tuple-element.54), channel_id=1, source_target_pairs={{0,8},{8,16},{16,24},{24,32},{32,40},{40,48},{48,56},{56,64},{64,7... | collective-permute-start | bytes 12296 | tf_op jit(solution)/shard_map/ppermute | solution.py:23
  125.7 0.8 collective-permute-done.33
  126.5 1.9 collective-permute-start.34
  128.4 5.0 %collective-permute-start.35 = (f32[4,1,64]{2,1,0:T(1,128)S(1)}, f32[4,1,64]{2,1,0:T(1,128)S(1)}, u32[]{:S(2)}, u32[]{:S(2)}) collective-permute-start(f32[4,1,64]{2,1,0:T(1,128)S(1)} %get-tuple-element.48), channel_id=1, source_target_pairs={{0,1},{1,2},{2,3},{3,4},{4,5},{5,6},{6,7},{8,9},{9,10},{10,11},{11... | collective-permute-start | bytes 3080 | tf_op jit(solution)/shard_map/ppermute | solution.py:23
  134.4 1.3 collective-permute-start.36
  135.7 6.4 %collective-permute-start.37 = (f32[1,16,64]{2,1,0:T(8,128)S(1)}, f32[1,16,64]{2,1,0:T(8,128)S(1)}, u32[]{:S(2)}, u32[]{:S(2)}) collective-permute-start(f32[1,16,64]{2,1,0:T(8,128)S(1)} %get-tuple-element.52), channel_id=1, source_target_pairs={{0,8},{8,16},{16,24},{24,32},{32,40},{40,48},{48,56},{56,64},{64,7... | collective-permute-start | bytes 12296 | tf_op jit(solution)/shard_map/ppermute | solution.py:23
  142.1 46.3 %all-gather.1 = f32[128,1,256]{2,1,0:T(1,128)S(1)} all-gather(f32[1,1,256]{2,1,0:T(1,128)S(1)} %reshape.304), channel_id=1, replica_groups=mesh['xb'=16,'yb'=8] {'xb','yb'}, dimensions={0}, use_global_device_ids=true | all-gather | bytes 132096 | tf_op jit(solution)/shard_map/all_gather | solution.py:122
  188.9 2.1 collective-permute-start.38
  190.9 3.5 %collective-permute-start.39 = (f32[4,1,64]{2,1,0:T(1,128)S(1)}, f32[4,1,64]{2,1,0:T(1,128)S(1)}, u32[]{:S(2)}, u32[]{:S(2)}) collective-permute-start(f32[4,1,64]{2,1,0:T(1,128)S(1)} %get-tuple-element.46), channel_id=1, source_target_pairs={{0,1},{1,2},{2,3},{3,4},{4,5},{5,6},{6,7},{8,9},{9,10},{10,11},{11... | collective-permute-start | bytes 3080 | tf_op jit(solution)/shard_map/ppermute | solution.py:23
  194.5 0.7 collective-permute-done.39
  195.7 34.0 %all-gather = f32[128,1,256]{2,1,0:T(1,128)S(1)} all-gather(f32[1,1,256]{2,1,0:T(1,128)S(1)} %reshape.302), channel_id=1, replica_groups=mesh['xb'=16,'yb'=8] {'xb','yb'}, dimensions={0}, use_global_device_ids=true | all-gather | bytes 132096 | tf_op jit(solution)/shard_map/all_gather | solution.py:121
  230.2 1.0 fusion.147
  231.2 0.7 fusion.23
  231.9 0.7 fusion.39
  232.5 0.7 fusion.55
  233.2 0.7 fusion.71
  233.9 0.7 fusion.87
  234.6 0.7 fusion.103
  235.3 0.7 fusion.119
  236.0 1.6 fusion.213
  239.0 0.6 dynamic-slice_add_fusion
  (110 shorter events, 8.2 us)
Async XLA Ops:
  0.6 20.8 %copy-start = (f32[8,64,256]{2,1,0:T(8,128)S(1)}, f32[8,64,256]{2,1,0:T(8,128)}, u32[]{:S(2)}) copy-start(f32[8,64,256]{2,1,0:T(8,128)} %param.5) | copy-start | bytes 1572868
  1.6 15.2 %collective-permute-start.1 = (f32[1,64,256]{2,1,0:T(8,128)S(1)}, f32[1,64,256]{2,1,0:T(8,128)S(1)}, u32[]{:S(2)}, u32[]{:S(2)}) collective-permute-start(f32[1,64,256]{2,1,0:T(8,128)S(1)} %get-tuple-element.31), channel_id=1, source_target_pairs={{0,8},{8,16},{16,24},{24,32},{32,40},{40,48},{48,56},{56,64},{64,7... | collective-permute-start | bytes 196616 | tf_op jit(solution)/shard_map/ppermute | solution.py:23
  6.0 15.5 %collective-permute-start = (f32[1,64,256]{2,1,0:T(8,128)S(1)}, f32[1,64,256]{2,1,0:T(8,128)S(1)}, u32[]{:S(2)}, u32[]{:S(2)}) collective-permute-start(f32[1,64,256]{2,1,0:T(8,128)S(1)} %get-tuple-element.30), channel_id=1, source_target_pairs={{8,0},{16,8},{24,16},{32,24},{40,32},{48,40},{56,48},{64,56},{72,6... | collective-permute-start | bytes 196616 | tf_op jit(solution)/shard_map/ppermute | solution.py:26
  8.1 17.2 %collective-permute-start.5 = (f32[1,64,256]{2,1,0:T(8,128)S(1)}, f32[1,64,256]{2,1,0:T(8,128)S(1)}, u32[]{:S(2)}, u32[]{:S(2)}) collective-permute-start(f32[1,64,256]{2,1,0:T(8,128)S(1)} %get-tuple-element.33), channel_id=1, source_target_pairs={{0,8},{8,16},{16,24},{24,32},{32,40},{40,48},{48,56},{56,64},{64,7... | collective-permute-start | bytes 196616 | tf_op jit(solution)/shard_map/ppermute | solution.py:23
  12.3 16.1 %collective-permute-start.4 = (f32[1,64,256]{2,1,0:T(8,128)S(1)}, f32[1,64,256]{2,1,0:T(8,128)S(1)}, u32[]{:S(2)}, u32[]{:S(2)}) collective-permute-start(f32[1,64,256]{2,1,0:T(8,128)S(1)} %get-tuple-element.32), channel_id=1, source_target_pairs={{8,0},{16,8},{24,16},{32,24},{40,32},{48,40},{56,48},{64,56},{72,6... | collective-permute-start | bytes 196616 | tf_op jit(solution)/shard_map/ppermute | solution.py:26
  13.7 14.7 %copy-start.3 = (f32[8,64,256]{2,1,0:T(8,128)S(1)}, f32[8,64,256]{2,1,0:T(8,128)}, u32[]{:S(2)}) copy-start(f32[8,64,256]{2,1,0:T(8,128)} %param.3) | copy-start | bytes 1572868
  15.3 43.6 %collective-permute-start.16 = (f32[1,32,128]{2,1,0:T(8,128)S(1)}, f32[1,32,128]{2,1,0:T(8,128)S(1)}, u32[]{:S(2)}, u32[]{:S(2)}) collective-permute-start(f32[1,32,128]{2,1,0:T(8,128)S(1)} %get-tuple-element.45), channel_id=1, source_target_pairs={{8,0},{16,8},{24,16},{32,24},{40,32},{48,40},{56,48},{64,56},{72,6... | collective-permute-start | bytes 49160 | tf_op jit(solution)/shard_map/ppermute | solution.py:26
  16.8 42.1 %collective-permute-start.17 = (f32[1,32,128]{2,1,0:T(8,128)S(1)}, f32[1,32,128]{2,1,0:T(8,128)S(1)}, u32[]{:S(2)}, u32[]{:S(2)}) collective-permute-start(f32[1,32,128]{2,1,0:T(8,128)S(1)} %get-tuple-element.44), channel_id=1, source_target_pairs={{0,8},{8,16},{16,24},{24,32},{32,40},{40,48},{48,56},{56,64},{64,7... | collective-permute-start | bytes 49160 | tf_op jit(solution)/shard_map/ppermute | solution.py:23
  21.5 8.9 %collective-permute-start.2 = (f32[10,1,256]{2,1,0:T(1,128)S(1)}, f32[10,1,256]{2,1,0:T(1,128)S(1)}, u32[]{:S(2)}, u32[]{:S(2)}) collective-permute-start(f32[10,1,256]{2,1,0:T(1,128)S(1)} %get-tuple-element.23), channel_id=1, source_target_pairs={{1,0},{2,1},{3,2},{4,3},{5,4},{6,5},{7,6},{9,8},{10,9},{11,10},{12... | collective-permute-start | bytes 30728 | tf_op jit(solution)/shard_map/ppermute | solution.py:26
  25.4 8.7 %collective-permute-start.3 = (f32[10,1,256]{2,1,0:T(1,128)S(1)}, f32[10,1,256]{2,1,0:T(1,128)S(1)}, u32[]{:S(2)}, u32[]{:S(2)}) collective-permute-start(f32[10,1,256]{2,1,0:T(1,128)S(1)} %get-tuple-element.22), channel_id=1, source_target_pairs={{0,1},{1,2},{2,3},{3,4},{4,5},{5,6},{6,7},{8,9},{9,10},{10,11},{11... | collective-permute-start | bytes 30728 | tf_op jit(solution)/shard_map/ppermute | solution.py:23
  28.5 6.1 %collective-permute-start.6 = (f32[10,1,256]{2,1,0:T(1,128)S(1)}, f32[10,1,256]{2,1,0:T(1,128)S(1)}, u32[]{:S(2)}, u32[]{:S(2)}) collective-permute-start(f32[10,1,256]{2,1,0:T(1,128)S(1)} %get-tuple-element.25), channel_id=1, source_target_pairs={{1,0},{2,1},{3,2},{4,3},{5,4},{6,5},{7,6},{9,8},{10,9},{11,10},{12... | collective-permute-start | bytes 30728 | tf_op jit(solution)/shard_map/ppermute | solution.py:26
  30.4 4.4 %collective-permute-start.7 = (f32[10,1,256]{2,1,0:T(1,128)S(1)}, f32[10,1,256]{2,1,0:T(1,128)S(1)}, u32[]{:S(2)}, u32[]{:S(2)}) collective-permute-start(f32[10,1,256]{2,1,0:T(1,128)S(1)} %get-tuple-element.24), channel_id=1, source_target_pairs={{0,1},{1,2},{2,3},{3,4},{4,5},{5,6},{6,7},{8,9},{9,10},{10,11},{11... | collective-permute-start | bytes 30728 | tf_op jit(solution)/shard_map/ppermute | solution.py:23
  34.6 1.0 copy-start.2
  36.8 5.6 %collective-permute-start.8 = (f32[1,64,256]{2,1,0:T(8,128)S(1)}, f32[1,64,256]{2,1,0:T(8,128)S(1)}, u32[]{:S(2)}, u32[]{:S(2)}) collective-permute-start(f32[1,64,256]{2,1,0:T(8,128)S(1)} %get-tuple-element.29), channel_id=1, source_target_pairs={{8,0},{16,8},{24,16},{32,24},{40,32},{48,40},{56,48},{64,56},{72,6... | collective-permute-start | bytes 196616 | tf_op jit(solution)/shard_map/ppermute | solution.py:26
  38.1 5.6 %collective-permute-start.9 = (f32[1,64,256]{2,1,0:T(8,128)S(1)}, f32[1,64,256]{2,1,0:T(8,128)S(1)}, u32[]{:S(2)}, u32[]{:S(2)}) collective-permute-start(f32[1,64,256]{2,1,0:T(8,128)S(1)} %get-tuple-element.28), channel_id=1, source_target_pairs={{0,8},{8,16},{16,24},{24,32},{32,40},{40,48},{48,56},{56,64},{64,7... | collective-permute-start | bytes 196616 | tf_op jit(solution)/shard_map/ppermute | solution.py:23
  43.7 6.9 %collective-permute-start.10 = (f32[10,1,256]{2,1,0:T(1,128)S(1)}, f32[10,1,256]{2,1,0:T(1,128)S(1)}, u32[]{:S(2)}, u32[]{:S(2)}) collective-permute-start(f32[10,1,256]{2,1,0:T(1,128)S(1)} %get-tuple-element.21), channel_id=1, source_target_pairs={{1,0},{2,1},{3,2},{4,3},{5,4},{6,5},{7,6},{9,8},{10,9},{11,10},{12... | collective-permute-start | bytes 30728 | tf_op jit(solution)/shard_map/ppermute | solution.py:26
  45.7 5.6 %collective-permute-start.11 = (f32[10,1,256]{2,1,0:T(1,128)S(1)}, f32[10,1,256]{2,1,0:T(1,128)S(1)}, u32[]{:S(2)}, u32[]{:S(2)}) collective-permute-start(f32[10,1,256]{2,1,0:T(1,128)S(1)} %get-tuple-element.20), channel_id=1, source_target_pairs={{0,1},{1,2},{2,3},{3,4},{4,5},{5,6},{6,7},{8,9},{9,10},{10,11},{11... | collective-permute-start | bytes 30728 | tf_op jit(solution)/shard_map/ppermute | solution.py:23
  52.9 19.3 %copy-start.1 = (f32[8,64,256]{2,1,0:T(8,128)}, f32[8,64,256]{2,1,0:T(8,128)S(1)}, u32[]{:S(2)}) copy-start(f32[8,64,256]{2,1,0:T(8,128)S(1)} %fusion.181) | copy-start | bytes 1572868
  53.0 12.4 %collective-permute-start.12 = (f32[1,64,256]{2,1,0:T(8,128)S(1)}, f32[1,64,256]{2,1,0:T(8,128)S(1)}, u32[]{:S(2)}, u32[]{:S(2)}) collective-permute-start(f32[1,64,256]{2,1,0:T(8,128)S(1)} %get-tuple-element.27), channel_id=1, source_target_pairs={{8,0},{16,8},{24,16},{32,24},{40,32},{48,40},{56,48},{64,56},{72,6... | collective-permute-start | bytes 196616 | tf_op jit(solution)/shard_map/ppermute | solution.py:26
  54.3 11.1 %collective-permute-start.13 = (f32[1,64,256]{2,1,0:T(8,128)S(1)}, f32[1,64,256]{2,1,0:T(8,128)S(1)}, u32[]{:S(2)}, u32[]{:S(2)}) collective-permute-start(f32[1,64,256]{2,1,0:T(8,128)S(1)} %get-tuple-element.26), channel_id=1, source_target_pairs={{0,8},{8,16},{16,24},{24,32},{32,40},{40,48},{48,56},{56,64},{64,7... | collective-permute-start | bytes 196616 | tf_op jit(solution)/shard_map/ppermute | solution.py:23
  58.9 12.0 %collective-permute-start.18 = (f32[6,1,128]{2,1,0:T(1,128)S(1)}, f32[6,1,128]{2,1,0:T(1,128)S(1)}, u32[]{:S(2)}, u32[]{:S(2)}) collective-permute-start(f32[6,1,128]{2,1,0:T(1,128)S(1)} %get-tuple-element.39), channel_id=1, source_target_pairs={{1,0},{2,1},{3,2},{4,3},{5,4},{6,5},{7,6},{9,8},{10,9},{11,10},{12... | collective-permute-start | bytes 9224 | tf_op jit(solution)/shard_map/ppermute | solution.py:26
  60.9 10.1 %collective-permute-start.19 = (f32[6,1,128]{2,1,0:T(1,128)S(1)}, f32[6,1,128]{2,1,0:T(1,128)S(1)}, u32[]{:S(2)}, u32[]{:S(2)}) collective-permute-start(f32[6,1,128]{2,1,0:T(1,128)S(1)} %get-tuple-element.38), channel_id=1, source_target_pairs={{0,1},{1,2},{2,3},{3,4},{4,5},{5,6},{6,7},{8,9},{9,10},{10,11},{11... | collective-permute-start | bytes 9224 | tf_op jit(solution)/shard_map/ppermute | solution.py:23
  65.4 5.8 %collective-permute-start.14 = (f32[10,1,256]{2,1,0:T(1,128)S(1)}, f32[10,1,256]{2,1,0:T(1,128)S(1)}, u32[]{:S(2)}, u32[]{:S(2)}) collective-permute-start(f32[10,1,256]{2,1,0:T(1,128)S(1)} %get-tuple-element.19), channel_id=1, source_target_pairs={{1,0},{2,1},{3,2},{4,3},{5,4},{6,5},{7,6},{9,8},{10,9},{11,10},{12... | collective-permute-start | bytes 30728 | tf_op jit(solution)/shard_map/ppermute | solution.py:26
  67.3 4.4 %collective-permute-start.15 = (f32[10,1,256]{2,1,0:T(1,128)S(1)}, f32[10,1,256]{2,1,0:T(1,128)S(1)}, u32[]{:S(2)}, u32[]{:S(2)}) collective-permute-start(f32[10,1,256]{2,1,0:T(1,128)S(1)} %get-tuple-element.18), channel_id=1, source_target_pairs={{0,1},{1,2},{2,3},{3,4},{4,5},{5,6},{6,7},{8,9},{9,10},{10,11},{11... | collective-permute-start | bytes 30728 | tf_op jit(solution)/shard_map/ppermute | solution.py:23
  73.9 14.9 %collective-permute-start.20 = (f32[1,32,128]{2,1,0:T(8,128)S(1)}, f32[1,32,128]{2,1,0:T(8,128)S(1)}, u32[]{:S(2)}, u32[]{:S(2)}) collective-permute-start(f32[1,32,128]{2,1,0:T(8,128)S(1)} %get-tuple-element.43), channel_id=1, source_target_pairs={{8,0},{16,8},{24,16},{32,24},{40,32},{48,40},{56,48},{64,56},{72,6... | collective-permute-start | bytes 49160 | tf_op jit(solution)/shard_map/ppermute | solution.py:26
  75.2 13.6 %collective-permute-start.21 = (f32[1,32,128]{2,1,0:T(8,128)S(1)}, f32[1,32,128]{2,1,0:T(8,128)S(1)}, u32[]{:S(2)}, u32[]{:S(2)}) collective-permute-start(f32[1,32,128]{2,1,0:T(8,128)S(1)} %get-tuple-element.42), channel_id=1, source_target_pairs={{0,8},{8,16},{16,24},{24,32},{32,40},{40,48},{48,56},{56,64},{64,7... | collective-permute-start | bytes 49160 | tf_op jit(solution)/shard_map/ppermute | solution.py:23
  81.1 23.5 %collective-permute-start.28 = (f32[1,16,64]{2,1,0:T(8,128)S(1)}, f32[1,16,64]{2,1,0:T(8,128)S(1)}, u32[]{:S(2)}, u32[]{:S(2)}) collective-permute-start(f32[1,16,64]{2,1,0:T(8,128)S(1)} %get-tuple-element.57), channel_id=1, source_target_pairs={{8,0},{16,8},{24,16},{32,24},{40,32},{48,40},{56,48},{64,56},{72,6... | collective-permute-start | bytes 12296 | tf_op jit(solution)/shard_map/ppermute | solution.py:26
  82.4 22.2 %collective-permute-start.29 = (f32[1,16,64]{2,1,0:T(8,128)S(1)}, f32[1,16,64]{2,1,0:T(8,128)S(1)}, u32[]{:S(2)}, u32[]{:S(2)}) collective-permute-start(f32[1,16,64]{2,1,0:T(8,128)S(1)} %get-tuple-element.56), channel_id=1, source_target_pairs={{0,8},{8,16},{16,24},{24,32},{32,40},{40,48},{48,56},{56,64},{64,7... | collective-permute-start | bytes 12296 | tf_op jit(solution)/shard_map/ppermute | solution.py:23
  88.8 6.8 %collective-permute-start.22 = (f32[6,1,128]{2,1,0:T(1,128)S(1)}, f32[6,1,128]{2,1,0:T(1,128)S(1)}, u32[]{:S(2)}, u32[]{:S(2)}) collective-permute-start(f32[6,1,128]{2,1,0:T(1,128)S(1)} %get-tuple-element.37), channel_id=1, source_target_pairs={{1,0},{2,1},{3,2},{4,3},{5,4},{6,5},{7,6},{9,8},{10,9},{11,10},{12... | collective-permute-start | bytes 9224 | tf_op jit(solution)/shard_map/ppermute | solution.py:26
  90.7 5.5 %collective-permute-start.23 = (f32[6,1,128]{2,1,0:T(1,128)S(1)}, f32[6,1,128]{2,1,0:T(1,128)S(1)}, u32[]{:S(2)}, u32[]{:S(2)}) collective-permute-start(f32[6,1,128]{2,1,0:T(1,128)S(1)} %get-tuple-element.36), channel_id=1, source_target_pairs={{0,1},{1,2},{2,3},{3,4},{4,5},{5,6},{6,7},{8,9},{9,10},{10,11},{11... | collective-permute-start | bytes 9224 | tf_op jit(solution)/shard_map/ppermute | solution.py:23
  96.5 92.1 %copy-start.4 = (f32[4,32,128]{2,1,0:T(8,128)}, f32[4,32,128]{2,1,0:T(8,128)S(1)}, u32[]{:S(2)}) copy-start(f32[4,32,128]{2,1,0:T(8,128)S(1)} %fusion.243) | copy-start | bytes 196612
  96.6 14.5 %collective-permute-start.24 = (f32[1,32,128]{2,1,0:T(8,128)S(1)}, f32[1,32,128]{2,1,0:T(8,128)S(1)}, u32[]{:S(2)}, u32[]{:S(2)}) collective-permute-start(f32[1,32,128]{2,1,0:T(8,128)S(1)} %get-tuple-element.41), channel_id=1, source_target_pairs={{8,0},{16,8},{24,16},{32,24},{40,32},{48,40},{56,48},{64,56},{72,6... | collective-permute-start | bytes 49160 | tf_op jit(solution)/shard_map/ppermute | solution.py:26
  97.9 13.2 %collective-permute-start.25 = (f32[1,32,128]{2,1,0:T(8,128)S(1)}, f32[1,32,128]{2,1,0:T(8,128)S(1)}, u32[]{:S(2)}, u32[]{:S(2)}) collective-permute-start(f32[1,32,128]{2,1,0:T(8,128)S(1)} %get-tuple-element.40), channel_id=1, source_target_pairs={{0,8},{8,16},{16,24},{24,32},{32,40},{40,48},{48,56},{56,64},{64,7... | collective-permute-start | bytes 49160 | tf_op jit(solution)/shard_map/ppermute | solution.py:23
  104.6 12.0 %collective-permute-start.30 = (f32[4,1,64]{2,1,0:T(1,128)S(1)}, f32[4,1,64]{2,1,0:T(1,128)S(1)}, u32[]{:S(2)}, u32[]{:S(2)}) collective-permute-start(f32[4,1,64]{2,1,0:T(1,128)S(1)} %get-tuple-element.51), channel_id=1, source_target_pairs={{1,0},{2,1},{3,2},{4,3},{5,4},{6,5},{7,6},{9,8},{10,9},{11,10},{12... | collective-permute-start | bytes 3080 | tf_op jit(solution)/shard_map/ppermute | solution.py:26
  106.6 10.1 %collective-permute-start.31 = (f32[4,1,64]{2,1,0:T(1,128)S(1)}, f32[4,1,64]{2,1,0:T(1,128)S(1)}, u32[]{:S(2)}, u32[]{:S(2)}) collective-permute-start(f32[4,1,64]{2,1,0:T(1,128)S(1)} %get-tuple-element.50), channel_id=1, source_target_pairs={{0,1},{1,2},{2,3},{3,4},{4,5},{5,6},{6,7},{8,9},{9,10},{10,11},{11... | collective-permute-start | bytes 3080 | tf_op jit(solution)/shard_map/ppermute | solution.py:23
  111.1 5.7 %collective-permute-start.26 = (f32[6,1,128]{2,1,0:T(1,128)S(1)}, f32[6,1,128]{2,1,0:T(1,128)S(1)}, u32[]{:S(2)}, u32[]{:S(2)}) collective-permute-start(f32[6,1,128]{2,1,0:T(1,128)S(1)} %get-tuple-element.35), channel_id=1, source_target_pairs={{1,0},{2,1},{3,2},{4,3},{5,4},{6,5},{7,6},{9,8},{10,9},{11,10},{12... | collective-permute-start | bytes 9224 | tf_op jit(solution)/shard_map/ppermute | solution.py:26
  113.0 4.4 %collective-permute-start.27 = (f32[6,1,128]{2,1,0:T(1,128)S(1)}, f32[6,1,128]{2,1,0:T(1,128)S(1)}, u32[]{:S(2)}, u32[]{:S(2)}) collective-permute-start(f32[6,1,128]{2,1,0:T(1,128)S(1)} %get-tuple-element.34), channel_id=1, source_target_pairs={{0,1},{1,2},{2,3},{3,4},{4,5},{5,6},{6,7},{8,9},{9,10},{10,11},{11... | collective-permute-start | bytes 9224 | tf_op jit(solution)/shard_map/ppermute | solution.py:23
  118.0 7.7 %collective-permute-start.32 = (f32[1,16,64]{2,1,0:T(8,128)S(1)}, f32[1,16,64]{2,1,0:T(8,128)S(1)}, u32[]{:S(2)}, u32[]{:S(2)}) collective-permute-start(f32[1,16,64]{2,1,0:T(8,128)S(1)} %get-tuple-element.55), channel_id=1, source_target_pairs={{8,0},{16,8},{24,16},{32,24},{40,32},{48,40},{56,48},{64,56},{72,6... | collective-permute-start | bytes 12296 | tf_op jit(solution)/shard_map/ppermute | solution.py:26
  119.3 7.2 %collective-permute-start.33 = (f32[1,16,64]{2,1,0:T(8,128)S(1)}, f32[1,16,64]{2,1,0:T(8,128)S(1)}, u32[]{:S(2)}, u32[]{:S(2)}) collective-permute-start(f32[1,16,64]{2,1,0:T(8,128)S(1)} %get-tuple-element.54), channel_id=1, source_target_pairs={{0,8},{8,16},{16,24},{24,32},{32,40},{40,48},{48,56},{56,64},{64,7... | collective-permute-start | bytes 12296 | tf_op jit(solution)/shard_map/ppermute | solution.py:23
  126.5 7.2 %collective-permute-start.34 = (f32[4,1,64]{2,1,0:T(1,128)S(1)}, f32[4,1,64]{2,1,0:T(1,128)S(1)}, u32[]{:S(2)}, u32[]{:S(2)}) collective-permute-start(f32[4,1,64]{2,1,0:T(1,128)S(1)} %get-tuple-element.49), channel_id=1, source_target_pairs={{1,0},{2,1},{3,2},{4,3},{5,4},{6,5},{7,6},{9,8},{10,9},{11,10},{12... | collective-permute-start | bytes 3080 | tf_op jit(solution)/shard_map/ppermute | solution.py:26
  128.4 5.8 %collective-permute-start.35 = (f32[4,1,64]{2,1,0:T(1,128)S(1)}, f32[4,1,64]{2,1,0:T(1,128)S(1)}, u32[]{:S(2)}, u32[]{:S(2)}) collective-permute-start(f32[4,1,64]{2,1,0:T(1,128)S(1)} %get-tuple-element.48), channel_id=1, source_target_pairs={{0,1},{1,2},{2,3},{3,4},{4,5},{5,6},{6,7},{8,9},{9,10},{10,11},{11... | collective-permute-start | bytes 3080 | tf_op jit(solution)/shard_map/ppermute | solution.py:23
  134.4 95.8 %copy-start.5 = (f32[2,16,64]{2,1,0:T(8,128)}, f32[2,16,64]{2,1,0:T(8,128)S(1)}, u32[]{:S(2)}) copy-start(f32[2,16,64]{2,1,0:T(8,128)S(1)} %fusion.296) | copy-start | bytes 24580
  134.4 54.4 %collective-permute-start.36 = (f32[1,16,64]{2,1,0:T(8,128)S(1)}, f32[1,16,64]{2,1,0:T(8,128)S(1)}, u32[]{:S(2)}, u32[]{:S(2)}) collective-permute-start(f32[1,16,64]{2,1,0:T(8,128)S(1)} %get-tuple-element.53), channel_id=1, source_target_pairs={{8,0},{16,8},{24,16},{32,24},{40,32},{48,40},{56,48},{64,56},{72,6... | collective-permute-start | bytes 12296 | tf_op jit(solution)/shard_map/ppermute | solution.py:26
  135.7 53.1 %collective-permute-start.37 = (f32[1,16,64]{2,1,0:T(8,128)S(1)}, f32[1,16,64]{2,1,0:T(8,128)S(1)}, u32[]{:S(2)}, u32[]{:S(2)}) collective-permute-start(f32[1,16,64]{2,1,0:T(8,128)S(1)} %get-tuple-element.52), channel_id=1, source_target_pairs={{0,8},{8,16},{16,24},{24,32},{32,40},{40,48},{48,56},{56,64},{64,7... | collective-permute-start | bytes 12296 | tf_op jit(solution)/shard_map/ppermute | solution.py:23
  188.9 5.6 %collective-permute-start.38 = (f32[4,1,64]{2,1,0:T(1,128)S(1)}, f32[4,1,64]{2,1,0:T(1,128)S(1)}, u32[]{:S(2)}, u32[]{:S(2)}) collective-permute-start(f32[4,1,64]{2,1,0:T(1,128)S(1)} %get-tuple-element.47), channel_id=1, source_target_pairs={{1,0},{2,1},{3,2},{4,3},{5,4},{6,5},{7,6},{9,8},{10,9},{11,10},{12... | collective-permute-start | bytes 3080 | tf_op jit(solution)/shard_map/ppermute | solution.py:26
  190.9 4.2 %collective-permute-start.39 = (f32[4,1,64]{2,1,0:T(1,128)S(1)}, f32[4,1,64]{2,1,0:T(1,128)S(1)}, u32[]{:S(2)}, u32[]{:S(2)}) collective-permute-start(f32[4,1,64]{2,1,0:T(1,128)S(1)} %get-tuple-element.46), channel_id=1, source_target_pairs={{0,1},{1,2},{2,3},{3,4},{4,5},{5,6},{6,7},{8,9},{9,10},{10,11},{11... | collective-permute-start | bytes 3080 | tf_op jit(solution)/shard_map/ppermute | solution.py:23
where the time goes:
time: 241 us; the launch traced here: 240 us
  starting transfers between devices  129 us (54%)
  blocking collectives  80.2 us (33%)
  other arithmetic  15.3 us (6%)
  waiting for transfers between devices  6.04 us (3%)
  matrix products  3.23 us (1%)
  between operations  3.06 us (1%)
  local copies, waits for them, and re-layouts  2.89 us (1%)
    ppermute x20, starting transfers between devices, with_halo(): lax.ppermute(lax.slice_in_dim(block, block.shape[dim] - width, None, axis...  94.7 us
    all_gather x1, blocking collectives, collect_grid(): lax.all_gather(coefficient.reshape(1, -1), ('xb', 'yb'), axis=0, tiled=True)  46.3 us
    ppermute x20, starting transfers between devices, with_halo(): lax.ppermute(lax.slice_in_dim(block, 0, width, axis=dim), axis, backward)  34.1 us
    all_gather x1, blocking collectives, collect_grid(): lax.all_gather(right_side.reshape(1, -1), ('xb', 'yb'), axis=0, tiled=True)  34 us
    ppermute x20, waiting for transfers between devices, with_halo(): lax.ppermute(lax.slice_in_dim(block, block.shape[dim] - width, None, axis...  5.99 us
  transfers between devices with their start and end apart: 40, of which 9 were waited for; matrix products, arithmetic and copies ran while one was open for 3% of the time, Pallas kernels for 0%

commit v1 on v0

--- a/solution.py
+++ b/solution.py
@@ -1,3 +1,4 @@
+import functools
 import jax
 import jax.numpy as jnp
 from jax import lax
@@ -13,6 +14,18 @@
 cheb_carry = cheb_second * cheb_first
 cheb_resid = 2.0 * cheb_second / cheb_delta
 jacobi_weight = 0.8
+
+
+def register_ladders(local_array, axis_id):
+    return jnp.concatenate(
+        lax.all_to_all(
+            jnp.stack([local_array for _ in range(lax.psum(1, axis_id))]), axis_id, 0, 0
+        ),
+        axis=0,
+    )
+
+
+order_thing = functools.partial(register_ladders, axis_id=("xb", "yb"))
 
 
 def with_halo(block, sides, width):
@@ -119,7 +132,7 @@
     count_y = lax.axis_size("yb")
     flat = (
         lax.all_gather(right_side.reshape(1, -1), ("xb", "yb"), axis=0, tiled=True),
-        lax.all_gather(coefficient.reshape(1, -1), ("xb", "yb"), axis=0, tiled=True),
+        order_thing(coefficient.reshape(1, -1)),
     )
     return tuple(
         (

time: 241 us -> 220 us (0.913)
  blocking collectives: 80.2 us -> 42.8 us
  starting transfers between devices: 129 us -> 145 us
    all_gather x1 -> x0, blocking collectives: 46.3 us -> none  [collect_grid(): lax.all_gather(coefficient.reshape(1, -1), ('xb', 'yb'), axis=0, tiled=True)]
    all_to_all x0 -> x1, starting transfers between devices: none -> 17.4 us  [register_ladders(): lax.all_to_all(jnp.stack([local_array for _ in range(lax.psum(1, axis_id)...]
    all_gather x1, blocking collectives: 34 us -> 42.8 us  [collect_grid(): lax.all_gather(right_side.reshape(1, -1), ('xb', 'yb'), axis=0, tiled=True)]
    ppermute x20, starting transfers between devices: 94.7 us -> 91.4 us  [with_halo(): lax.ppermute(lax.slice_in_dim(block, block.shape[dim] - width, None, axis...]
  transfers between devices with their start and end apart: 40 -> 41, of which waited for: 9 -> 9; matrix products, arithmetic and copies ran while one was open for 3% -> 4% of each run, Pallas kernels for 0% -> 0%
where the time goes in v1:
time: 220 us; the launch traced here: 219 us
  starting transfers between devices  145 us (66%)
  blocking collectives  42.8 us (19%)
  other arithmetic  15.3 us (7%)
  waiting for transfers between devices  5.8 us (3%)
  local copies, waits for them, and re-layouts  3.63 us (2%)
  matrix products  3.23 us (1%)
  between operations  2.96 us (1%)
    ppermute x20, starting transfers between devices, with_halo(): lax.ppermute(lax.slice_in_dim(block, block.shape[dim] - width, None, axis...  91.4 us
    all_gather x1, blocking collectives, collect_grid(): lax.all_gather(right_side.reshape(1, -1), ('xb', 'yb'), axis=0, tiled=True)  42.8 us
    ppermute x20, starting transfers between devices, with_halo(): lax.ppermute(lax.slice_in_dim(block, 0, width, axis=dim), axis, backward)  36.1 us
    all_to_all x1, starting transfers between devices, register_ladders(): lax.all_to_all(jnp.stack([local_array for _ in range(lax.psum(1, axis_id)...  17.4 us
    ppermute x20, waiting for transfers between devices, with_halo(): lax.ppermute(lax.slice_in_dim(block, block.shape[dim] - width, None, axis...  5.75 us
    add x7, other arithmetic, coarse_solve(): field + jacobi_weight * (right_side - apply_operator(extend(field), field...  4.78 us
  transfers between devices with their start and end apart: 41, of which 9 were waited for; matrix products, arithmetic and copies ran while one was open for 4% of the time, Pallas kernels for 0%

profile of v1, /device:TPU:1, one launch (start us, length us, event | category | flops | bytes accessed | tf_op | source)
XLA Modules:
  0.0 218.6 jit_solution(17982482382873073655)
XLA Ops:
  0.6 0.9 fusion.348
  1.6 4.4 %collective-permute-start.1 = (f32[1,64,256]{2,1,0:T(8,128)S(1)}, f32[1,64,256]{2,1,0:T(8,128)S(1)}, u32[]{:S(2)}, u32[]{:S(2)}) collective-permute-start(f32[1,64,256]{2,1,0:T(8,128)S(1)} %get-tuple-element.31), channel_id=1, source_target_pairs={{0,8},{8,16},{16,24},{24,32},{32,40},{40,48},{48,56},{56,64},{64,7... | collective-permute-start | bytes 196616 | tf_op jit(solution)/shard_map/ppermute | solution.py:36
  6.0 1.3 collective-permute-start
  7.3 0.9 fusion.349
  8.1 4.2 %collective-permute-start.5 = (f32[1,64,256]{2,1,0:T(8,128)S(1)}, f32[1,64,256]{2,1,0:T(8,128)S(1)}, u32[]{:S(2)}, u32[]{:S(2)}) collective-permute-start(f32[1,64,256]{2,1,0:T(8,128)S(1)} %get-tuple-element.33), channel_id=1, source_target_pairs={{0,8},{8,16},{16,24},{24,32},{32,40},{40,48},{48,56},{56,64},{64,7... | collective-permute-start | bytes 196616 | tf_op jit(solution)/shard_map/ppermute | solution.py:36
  12.3 1.3 collective-permute-start.4
  13.7 1.4 fusion.217
  15.3 1.3 collective-permute-start.16
  16.8 4.6 %collective-permute-start.17 = (f32[1,32,128]{2,1,0:T(8,128)S(1)}, f32[1,32,128]{2,1,0:T(8,128)S(1)}, u32[]{:S(2)}, u32[]{:S(2)}) collective-permute-start(f32[1,32,128]{2,1,0:T(8,128)S(1)} %get-tuple-element.44), channel_id=1, source_target_pairs={{0,8},{8,16},{16,24},{24,32},{32,40},{40,48},{48,56},{56,64},{64,7... | collective-permute-start | bytes 49160 | tf_op jit(solution)/shard_map/ppermute | solution.py:36
  21.5 3.8 %collective-permute-start.2 = (f32[10,1,256]{2,1,0:T(1,128)S(1)}, f32[10,1,256]{2,1,0:T(1,128)S(1)}, u32[]{:S(2)}, u32[]{:S(2)}) collective-permute-start(f32[10,1,256]{2,1,0:T(1,128)S(1)} %get-tuple-element.23), channel_id=1, source_target_pairs={{1,0},{2,1},{3,2},{4,3},{5,4},{6,5},{7,6},{9,8},{10,9},{11,10},{12... | collective-permute-start | bytes 30728 | tf_op jit(solution)/shard_map/ppermute | solution.py:39
  25.4 3.0 %collective-permute-start.3 = (f32[10,1,256]{2,1,0:T(1,128)S(1)}, f32[10,1,256]{2,1,0:T(1,128)S(1)}, u32[]{:S(2)}, u32[]{:S(2)}) collective-permute-start(f32[10,1,256]{2,1,0:T(1,128)S(1)} %get-tuple-element.22), channel_id=1, source_target_pairs={{0,1},{1,2},{2,3},{3,4},{4,5},{5,6},{6,7},{8,9},{9,10},{10,11},{11... | collective-permute-start | bytes 30728 | tf_op jit(solution)/shard_map/ppermute | solution.py:36
  28.5 1.9 collective-permute-start.6
  30.4 3.6 %collective-permute-start.7 = (f32[10,1,256]{2,1,0:T(1,128)S(1)}, f32[10,1,256]{2,1,0:T(1,128)S(1)}, u32[]{:S(2)}, u32[]{:S(2)}) collective-permute-start(f32[10,1,256]{2,1,0:T(1,128)S(1)} %get-tuple-element.24), channel_id=1, source_target_pairs={{0,1},{1,2},{2,3},{3,4},{4,5},{5,6},{6,7},{8,9},{9,10},{10,11},{11... | collective-permute-start | bytes 30728 | tf_op jit(solution)/shard_map/ppermute | solution.py:36
  35.6 1.2 fusion.342
  36.8 1.3 collective-permute-start.8
  38.1 4.3 %collective-permute-start.9 = (f32[1,64,256]{2,1,0:T(8,128)S(1)}, f32[1,64,256]{2,1,0:T(8,128)S(1)}, u32[]{:S(2)}, u32[]{:S(2)}) collective-permute-start(f32[1,64,256]{2,1,0:T(8,128)S(1)} %get-tuple-element.28), channel_id=1, source_target_pairs={{0,8},{8,16},{16,24},{24,32},{32,40},{40,48},{48,56},{56,64},{64,7... | collective-permute-start | bytes 196616 | tf_op jit(solution)/shard_map/ppermute | solution.py:36
  42.4 1.3 collective-permute-done.9
  43.7 1.9 collective-permute-start.10
  45.7 4.8 %collective-permute-start.11 = (f32[10,1,256]{2,1,0:T(1,128)S(1)}, f32[10,1,256]{2,1,0:T(1,128)S(1)}, u32[]{:S(2)}, u32[]{:S(2)}) collective-permute-start(f32[10,1,256]{2,1,0:T(1,128)S(1)} %get-tuple-element.20), channel_id=1, source_target_pairs={{0,1},{1,2},{2,3},{3,4},{4,5},{5,6},{6,7},{8,9},{9,10},{10,11},{11... | collective-permute-start | bytes 30728 | tf_op jit(solution)/shard_map/ppermute | solution.py:36
  50.6 0.6 collective-permute-done.11
  51.7 1.2 fusion.181
  53.0 1.3 collective-permute-start.12
  54.3 4.6 %collective-permute-start.13 = (f32[1,64,256]{2,1,0:T(8,128)S(1)}, f32[1,64,256]{2,1,0:T(8,128)S(1)}, u32[]{:S(2)}, u32[]{:S(2)}) collective-permute-start(f32[1,64,256]{2,1,0:T(8,128)S(1)} %get-tuple-element.26), channel_id=1, source_target_pairs={{0,8},{8,16},{16,24},{24,32},{32,40},{40,48},{48,56},{56,64},{64,7... | collective-permute-start | bytes 196616 | tf_op jit(solution)/shard_map/ppermute | solution.py:36
  58.9 1.9 collective-permute-start.18
  60.9 4.5 %collective-permute-start.19 = (f32[6,1,128]{2,1,0:T(1,128)S(1)}, f32[6,1,128]{2,1,0:T(1,128)S(1)}, u32[]{:S(2)}, u32[]{:S(2)}) collective-permute-start(f32[6,1,128]{2,1,0:T(1,128)S(1)} %get-tuple-element.38), channel_id=1, source_target_pairs={{0,1},{1,2},{2,3},{3,4},{4,5},{5,6},{6,7},{8,9},{9,10},{10,11},{11... | collective-permute-start | bytes 9224 | tf_op jit(solution)/shard_map/ppermute | solution.py:36
  65.4 1.9 collective-permute-start.14
  67.3 3.6 %collective-permute-start.15 = (f32[10,1,256]{2,1,0:T(1,128)S(1)}, f32[10,1,256]{2,1,0:T(1,128)S(1)}, u32[]{:S(2)}, u32[]{:S(2)}) collective-permute-start(f32[10,1,256]{2,1,0:T(1,128)S(1)} %get-tuple-element.18), channel_id=1, source_target_pairs={{0,1},{1,2},{2,3},{3,4},{4,5},{5,6},{6,7},{8,9},{9,10},{10,11},{11... | collective-permute-start | bytes 30728 | tf_op jit(solution)/shard_map/ppermute | solution.py:36
  72.2 1.1 fusion.166
  73.9 1.3 collective-permute-start.20
  75.2 5.8 %collective-permute-start.21 = (f32[1,32,128]{2,1,0:T(8,128)S(1)}, f32[1,32,128]{2,1,0:T(8,128)S(1)}, u32[]{:S(2)}, u32[]{:S(2)}) collective-permute-start(f32[1,32,128]{2,1,0:T(8,128)S(1)} %get-tuple-element.42), channel_id=1, source_target_pairs={{0,8},{8,16},{16,24},{24,32},{32,40},{40,48},{48,56},{56,64},{64,7... | collective-permute-start | bytes 49160 | tf_op jit(solution)/shard_map/ppermute | solution.py:36
  81.1 1.3 collective-permute-start.28
  82.4 6.4 %collective-permute-start.29 = (f32[1,16,64]{2,1,0:T(8,128)S(1)}, f32[1,16,64]{2,1,0:T(8,128)S(1)}, u32[]{:S(2)}, u32[]{:S(2)}) collective-permute-start(f32[1,16,64]{2,1,0:T(8,128)S(1)} %get-tuple-element.56), channel_id=1, source_target_pairs={{0,8},{8,16},{16,24},{24,32},{32,40},{40,48},{48,56},{56,64},{64,7... | collective-permute-start | bytes 12296 | tf_op jit(solution)/shard_map/ppermute | solution.py:36
  88.8 1.9 collective-permute-start.22
  90.7 4.8 %collective-permute-start.23 = (f32[6,1,128]{2,1,0:T(1,128)S(1)}, f32[6,1,128]{2,1,0:T(1,128)S(1)}, u32[]{:S(2)}, u32[]{:S(2)}) collective-permute-start(f32[6,1,128]{2,1,0:T(1,128)S(1)} %get-tuple-element.36), channel_id=1, source_target_pairs={{0,1},{1,2},{2,3},{3,4},{4,5},{5,6},{6,7},{8,9},{9,10},{10,11},{11... | collective-permute-start | bytes 9224 | tf_op jit(solution)/shard_map/ppermute | solution.py:36
  95.6 0.6 collective-permute-done.23
  96.6 1.3 collective-permute-start.24
  97.9 6.7 %collective-permute-start.25 = (f32[1,32,128]{2,1,0:T(8,128)S(1)}, f32[1,32,128]{2,1,0:T(8,128)S(1)}, u32[]{:S(2)}, u32[]{:S(2)}) collective-permute-start(f32[1,32,128]{2,1,0:T(8,128)S(1)} %get-tuple-element.40), channel_id=1, source_target_pairs={{0,8},{8,16},{16,24},{24,32},{32,40},{40,48},{48,56},{56,64},{64,7... | collective-permute-start | bytes 49160 | tf_op jit(solution)/shard_map/ppermute | solution.py:36
  104.6 1.9 collective-permute-start.30
  106.6 4.5 %collective-permute-start.31 = (f32[4,1,64]{2,1,0:T(1,128)S(1)}, f32[4,1,64]{2,1,0:T(1,128)S(1)}, u32[]{:S(2)}, u32[]{:S(2)}) collective-permute-start(f32[4,1,64]{2,1,0:T(1,128)S(1)} %get-tuple-element.50), channel_id=1, source_target_pairs={{0,1},{1,2},{2,3},{3,4},{4,5},{5,6},{6,7},{8,9},{9,10},{10,11},{11... | collective-permute-start | bytes 3080 | tf_op jit(solution)/shard_map/ppermute | solution.py:36
  111.1 1.9 collective-permute-start.26
  113.0 3.6 %collective-permute-start.27 = (f32[6,1,128]{2,1,0:T(1,128)S(1)}, f32[6,1,128]{2,1,0:T(1,128)S(1)}, u32[]{:S(2)}, u32[]{:S(2)}) collective-permute-start(f32[6,1,128]{2,1,0:T(1,128)S(1)} %get-tuple-element.34), channel_id=1, source_target_pairs={{0,1},{1,2},{2,3},{3,4},{4,5},{5,6},{6,7},{8,9},{9,10},{10,11},{11... | collective-permute-start | bytes 9224 | tf_op jit(solution)/shard_map/ppermute | solution.py:36
  118.0 1.3 collective-permute-start.32
  119.3 6.4 %collective-permute-start.33 = (f32[1,16,64]{2,1,0:T(8,128)S(1)}, f32[1,16,64]{2,1,0:T(8,128)S(1)}, u32[]{:S(2)}, u32[]{:S(2)}) collective-permute-start(f32[1,16,64]{2,1,0:T(8,128)S(1)} %get-tuple-element.54), channel_id=1, source_target_pairs={{0,8},{8,16},{16,24},{24,32},{32,40},{40,48},{48,56},{56,64},{64,7... | collective-permute-start | bytes 12296 | tf_op jit(solution)/shard_map/ppermute | solution.py:36
  125.7 0.8 collective-permute-done.33
  126.5 1.9 collective-permute-start.34
  128.4 5.0 %collective-permute-start.35 = (f32[4,1,64]{2,1,0:T(1,128)S(1)}, f32[4,1,64]{2,1,0:T(1,128)S(1)}, u32[]{:S(2)}, u32[]{:S(2)}) collective-permute-start(f32[4,1,64]{2,1,0:T(1,128)S(1)} %get-tuple-element.48), channel_id=1, source_target_pairs={{0,1},{1,2},{2,3},{3,4},{4,5},{5,6},{6,7},{8,9},{9,10},{10,11},{11... | collective-permute-start | bytes 3080 | tf_op jit(solution)/shard_map/ppermute | solution.py:36
  133.7 0.7 stack.3
  134.4 17.4 %all-to-all-start = ((f32[128,1,256]{2,1,0:T(1,128)}), f32[128,1,256]{2,1,0:T(1,128)S(1)}, u32[]{:S(2)}, u32[]{:S(2)}) async-start(f32[128,1,256]{2,1,0:T(1,128)} %stack.3), calls=%async_computation | async-start | bytes 262144 | tf_op jit(solution)/shard_map/all_to_all | solution.py:21
  152.1 1.3 collective-permute-start.36
  153.4 4.0 %collective-permute-start.37 = (f32[1,16,64]{2,1,0:T(8,128)S(1)}, f32[1,16,64]{2,1,0:T(8,128)S(1)}, u32[]{:S(2)}, u32[]{:S(2)}) collective-permute-start(f32[1,16,64]{2,1,0:T(8,128)S(1)} %get-tuple-element.52), channel_id=1, source_target_pairs={{0,8},{8,16},{16,24},{24,32},{32,40},{40,48},{48,56},{56,64},{64,7... | collective-permute-start | bytes 12296 | tf_op jit(solution)/shard_map/ppermute | solution.py:36
  157.4 0.8 collective-permute-done.37
  158.2 4.1 %collective-permute-start.38 = (f32[4,1,64]{2,1,0:T(1,128)S(1)}, f32[4,1,64]{2,1,0:T(1,128)S(1)}, u32[]{:S(2)}, u32[]{:S(2)}) collective-permute-start(f32[4,1,64]{2,1,0:T(1,128)S(1)} %get-tuple-element.47), channel_id=1, source_target_pairs={{1,0},{2,1},{3,2},{4,3},{5,4},{6,5},{7,6},{9,8},{10,9},{11,10},{12... | collective-permute-start | bytes 3080 | tf_op jit(solution)/shard_map/ppermute | solution.py:39
  162.3 2.5 %collective-permute-start.39 = (f32[4,1,64]{2,1,0:T(1,128)S(1)}, f32[4,1,64]{2,1,0:T(1,128)S(1)}, u32[]{:S(2)}, u32[]{:S(2)}) collective-permute-start(f32[4,1,64]{2,1,0:T(1,128)S(1)} %get-tuple-element.46), channel_id=1, source_target_pairs={{0,1},{1,2},{2,3},{3,4},{4,5},{5,6},{6,7},{8,9},{9,10},{10,11},{11... | collective-permute-start | bytes 3080 | tf_op jit(solution)/shard_map/ppermute | solution.py:36
  166.0 42.8 %all-gather = f32[128,1,256]{2,1,0:T(1,128)S(1)} all-gather(f32[1,1,256]{2,1,0:T(1,128)S(1)} %reshape.302), channel_id=1, replica_groups=mesh['xb'=16,'yb'=8] {'xb','yb'}, dimensions={0}, use_global_device_ids=true | all-gather | bytes 132096 | tf_op jit(solution)/shard_map/all_gather | solution.py:134
  209.4 1.0 fusion.147
  210.4 0.7 fusion.23
  211.0 0.7 fusion.39
  211.7 0.7 fusion.55
  212.4 0.7 fusion.71
  213.1 0.7 fusion.87
  213.8 0.7 fusion.103
  214.5 0.7 fusion.119
  215.2 1.6 fusion.213
  218.0 0.6 dynamic-slice_add_fusion
  (112 shorter events, 8.5 us)
Async XLA Ops:
  0.6 20.8 %copy-start = (f32[8,64,256]{2,1,0:T(8,128)S(1)}, f32[8,64,256]{2,1,0:T(8,128)}, u32[]{:S(2)}) copy-start(f32[8,64,256]{2,1,0:T(8,128)} %param.5) | copy-start | bytes 1572868
  1.6 15.2 %collective-permute-start.1 = (f32[1,64,256]{2,1,0:T(8,128)S(1)}, f32[1,64,256]{2,1,0:T(8,128)S(1)}, u32[]{:S(2)}, u32[]{:S(2)}) collective-permute-start(f32[1,64,256]{2,1,0:T(8,128)S(1)} %get-tuple-element.31), channel_id=1, source_target_pairs={{0,8},{8,16},{16,24},{24,32},{32,40},{40,48},{48,56},{56,64},{64,7... | collective-permute-start | bytes 196616 | tf_op jit(solution)/shard_map/ppermute | solution.py:36
  6.0 15.5 %collective-permute-start = (f32[1,64,256]{2,1,0:T(8,128)S(1)}, f32[1,64,256]{2,1,0:T(8,128)S(1)}, u32[]{:S(2)}, u32[]{:S(2)}) collective-permute-start(f32[1,64,256]{2,1,0:T(8,128)S(1)} %get-tuple-element.30), channel_id=1, source_target_pairs={{8,0},{16,8},{24,16},{32,24},{40,32},{48,40},{56,48},{64,56},{72,6... | collective-permute-start | bytes 196616 | tf_op jit(solution)/shard_map/ppermute | solution.py:39
  8.1 17.2 %collective-permute-start.5 = (f32[1,64,256]{2,1,0:T(8,128)S(1)}, f32[1,64,256]{2,1,0:T(8,128)S(1)}, u32[]{:S(2)}, u32[]{:S(2)}) collective-permute-start(f32[1,64,256]{2,1,0:T(8,128)S(1)} %get-tuple-element.33), channel_id=1, source_target_pairs={{0,8},{8,16},{16,24},{24,32},{32,40},{40,48},{48,56},{56,64},{64,7... | collective-permute-start | bytes 196616 | tf_op jit(solution)/shard_map/ppermute | solution.py:36
  12.3 16.1 %collective-permute-start.4 = (f32[1,64,256]{2,1,0:T(8,128)S(1)}, f32[1,64,256]{2,1,0:T(8,128)S(1)}, u32[]{:S(2)}, u32[]{:S(2)}) collective-permute-start(f32[1,64,256]{2,1,0:T(8,128)S(1)} %get-tuple-element.32), channel_id=1, source_target_pairs={{8,0},{16,8},{24,16},{32,24},{40,32},{48,40},{56,48},{64,56},{72,6... | collective-permute-start | bytes 196616 | tf_op jit(solution)/shard_map/ppermute | solution.py:39
  13.7 14.7 %copy-start.3 = (f32[8,64,256]{2,1,0:T(8,128)S(1)}, f32[8,64,256]{2,1,0:T(8,128)}, u32[]{:S(2)}) copy-start(f32[8,64,256]{2,1,0:T(8,128)} %param.3) | copy-start | bytes 1572868
  15.3 43.6 %collective-permute-start.16 = (f32[1,32,128]{2,1,0:T(8,128)S(1)}, f32[1,32,128]{2,1,0:T(8,128)S(1)}, u32[]{:S(2)}, u32[]{:S(2)}) collective-permute-start(f32[1,32,128]{2,1,0:T(8,128)S(1)} %get-tuple-element.45), channel_id=1, source_target_pairs={{8,0},{16,8},{24,16},{32,24},{40,32},{48,40},{56,48},{64,56},{72,6... | collective-permute-start | bytes 49160 | tf_op jit(solution)/shard_map/ppermute | solution.py:39
  16.8 42.1 %collective-permute-start.17 = (f32[1,32,128]{2,1,0:T(8,128)S(1)}, f32[1,32,128]{2,1,0:T(8,128)S(1)}, u32[]{:S(2)}, u32[]{:S(2)}) collective-permute-start(f32[1,32,128]{2,1,0:T(8,128)S(1)} %get-tuple-element.44), channel_id=1, source_target_pairs={{0,8},{8,16},{16,24},{24,32},{32,40},{40,48},{48,56},{56,64},{64,7... | collective-permute-start | bytes 49160 | tf_op jit(solution)/shard_map/ppermute | solution.py:36
  21.5 8.9 %collective-permute-start.2 = (f32[10,1,256]{2,1,0:T(1,128)S(1)}, f32[10,1,256]{2,1,0:T(1,128)S(1)}, u32[]{:S(2)}, u32[]{:S(2)}) collective-permute-start(f32[10,1,256]{2,1,0:T(1,128)S(1)} %get-tuple-element.23), channel_id=1, source_target_pairs={{1,0},{2,1},{3,2},{4,3},{5,4},{6,5},{7,6},{9,8},{10,9},{11,10},{12... | collective-permute-start | bytes 30728 | tf_op jit(solution)/shard_map/ppermute | solution.py:39
  25.4 8.7 %collective-permute-start.3 = (f32[10,1,256]{2,1,0:T(1,128)S(1)}, f32[10,1,256]{2,1,0:T(1,128)S(1)}, u32[]{:S(2)}, u32[]{:S(2)}) collective-permute-start(f32[10,1,256]{2,1,0:T(1,128)S(1)} %get-tuple-element.22), channel_id=1, source_target_pairs={{0,1},{1,2},{2,3},{3,4},{4,5},{5,6},{6,7},{8,9},{9,10},{10,11},{11... | collective-permute-start | bytes 30728 | tf_op jit(solution)/shard_map/ppermute | solution.py:36
  28.5 6.1 %collective-permute-start.6 = (f32[10,1,256]{2,1,0:T(1,128)S(1)}, f32[10,1,256]{2,1,0:T(1,128)S(1)}, u32[]{:S(2)}, u32[]{:S(2)}) collective-permute-start(f32[10,1,256]{2,1,0:T(1,128)S(1)} %get-tuple-element.25), channel_id=1, source_target_pairs={{1,0},{2,1},{3,2},{4,3},{5,4},{6,5},{7,6},{9,8},{10,9},{11,10},{12... | collective-permute-start | bytes 30728 | tf_op jit(solution)/shard_map/ppermute | solution.py:39
  30.4 4.4 %collective-permute-start.7 = (f32[10,1,256]{2,1,0:T(1,128)S(1)}, f32[10,1,256]{2,1,0:T(1,128)S(1)}, u32[]{:S(2)}, u32[]{:S(2)}) collective-permute-start(f32[10,1,256]{2,1,0:T(1,128)S(1)} %get-tuple-element.24), channel_id=1, source_target_pairs={{0,1},{1,2},{2,3},{3,4},{4,5},{5,6},{6,7},{8,9},{9,10},{10,11},{11... | collective-permute-start | bytes 30728 | tf_op jit(solution)/shard_map/ppermute | solution.py:36
  34.6 1.0 copy-start.2
  36.8 5.6 %collective-permute-start.8 = (f32[1,64,256]{2,1,0:T(8,128)S(1)}, f32[1,64,256]{2,1,0:T(8,128)S(1)}, u32[]{:S(2)}, u32[]{:S(2)}) collective-permute-start(f32[1,64,256]{2,1,0:T(8,128)S(1)} %get-tuple-element.29), channel_id=1, source_target_pairs={{8,0},{16,8},{24,16},{32,24},{40,32},{48,40},{56,48},{64,56},{72,6... | collective-permute-start | bytes 196616 | tf_op jit(solution)/shard_map/ppermute | solution.py:39
  38.1 5.6 %collective-permute-start.9 = (f32[1,64,256]{2,1,0:T(8,128)S(1)}, f32[1,64,256]{2,1,0:T(8,128)S(1)}, u32[]{:S(2)}, u32[]{:S(2)}) collective-permute-start(f32[1,64,256]{2,1,0:T(8,128)S(1)} %get-tuple-element.28), channel_id=1, source_target_pairs={{0,8},{8,16},{16,24},{24,32},{32,40},{40,48},{48,56},{56,64},{64,7... | collective-permute-start | bytes 196616 | tf_op jit(solution)/shard_map/ppermute | solution.py:36
  43.7 6.9 %collective-permute-start.10 = (f32[10,1,256]{2,1,0:T(1,128)S(1)}, f32[10,1,256]{2,1,0:T(1,128)S(1)}, u32[]{:S(2)}, u32[]{:S(2)}) collective-permute-start(f32[10,1,256]{2,1,0:T(1,128)S(1)} %get-tuple-element.21), channel_id=1, source_target_pairs={{1,0},{2,1},{3,2},{4,3},{5,4},{6,5},{7,6},{9,8},{10,9},{11,10},{12... | collective-permute-start | bytes 30728 | tf_op jit(solution)/shard_map/ppermute | solution.py:39
  45.7 5.6 %collective-permute-start.11 = (f32[10,1,256]{2,1,0:T(1,128)S(1)}, f32[10,1,256]{2,1,0:T(1,128)S(1)}, u32[]{:S(2)}, u32[]{:S(2)}) collective-permute-start(f32[10,1,256]{2,1,0:T(1,128)S(1)} %get-tuple-element.20), channel_id=1, source_target_pairs={{0,1},{1,2},{2,3},{3,4},{4,5},{5,6},{6,7},{8,9},{9,10},{10,11},{11... | collective-permute-start | bytes 30728 | tf_op jit(solution)/shard_map/ppermute | solution.py:36
  52.9 19.3 %copy-start.1 = (f32[8,64,256]{2,1,0:T(8,128)}, f32[8,64,256]{2,1,0:T(8,128)S(1)}, u32[]{:S(2)}) copy-start(f32[8,64,256]{2,1,0:T(8,128)S(1)} %fusion.181) | copy-start | bytes 1572868
  53.0 12.4 %collective-permute-start.12 = (f32[1,64,256]{2,1,0:T(8,128)S(1)}, f32[1,64,256]{2,1,0:T(8,128)S(1)}, u32[]{:S(2)}, u32[]{:S(2)}) collective-permute-start(f32[1,64,256]{2,1,0:T(8,128)S(1)} %get-tuple-element.27), channel_id=1, source_target_pairs={{8,0},{16,8},{24,16},{32,24},{40,32},{48,40},{56,48},{64,56},{72,6... | collective-permute-start | bytes 196616 | tf_op jit(solution)/shard_map/ppermute | solution.py:39
  54.3 11.1 %collective-permute-start.13 = (f32[1,64,256]{2,1,0:T(8,128)S(1)}, f32[1,64,256]{2,1,0:T(8,128)S(1)}, u32[]{:S(2)}, u32[]{:S(2)}) collective-permute-start(f32[1,64,256]{2,1,0:T(8,128)S(1)} %get-tuple-element.26), channel_id=1, source_target_pairs={{0,8},{8,16},{16,24},{24,32},{32,40},{40,48},{48,56},{56,64},{64,7... | collective-permute-start | bytes 196616 | tf_op jit(solution)/shard_map/ppermute | solution.py:36
  58.9 12.0 %collective-permute-start.18 = (f32[6,1,128]{2,1,0:T(1,128)S(1)}, f32[6,1,128]{2,1,0:T(1,128)S(1)}, u32[]{:S(2)}, u32[]{:S(2)}) collective-permute-start(f32[6,1,128]{2,1,0:T(1,128)S(1)} %get-tuple-element.39), channel_id=1, source_target_pairs={{1,0},{2,1},{3,2},{4,3},{5,4},{6,5},{7,6},{9,8},{10,9},{11,10},{12... | collective-permute-start | bytes 9224 | tf_op jit(solution)/shard_map/ppermute | solution.py:39
  60.9 10.1 %collective-permute-start.19 = (f32[6,1,128]{2,1,0:T(1,128)S(1)}, f32[6,1,128]{2,1,0:T(1,128)S(1)}, u32[]{:S(2)}, u32[]{:S(2)}) collective-permute-start(f32[6,1,128]{2,1,0:T(1,128)S(1)} %get-tuple-element.38), channel_id=1, source_target_pairs={{0,1},{1,2},{2,3},{3,4},{4,5},{5,6},{6,7},{8,9},{9,10},{10,11},{11... | collective-permute-start | bytes 9224 | tf_op jit(solution)/shard_map/ppermute | solution.py:36
  65.4 5.8 %collective-permute-start.14 = (f32[10,1,256]{2,1,0:T(1,128)S(1)}, f32[10,1,256]{2,1,0:T(1,128)S(1)}, u32[]{:S(2)}, u32[]{:S(2)}) collective-permute-start(f32[10,1,256]{2,1,0:T(1,128)S(1)} %get-tuple-element.19), channel_id=1, source_target_pairs={{1,0},{2,1},{3,2},{4,3},{5,4},{6,5},{7,6},{9,8},{10,9},{11,10},{12... | collective-permute-start | bytes 30728 | tf_op jit(solution)/shard_map/ppermute | solution.py:39
  67.3 4.4 %collective-permute-start.15 = (f32[10,1,256]{2,1,0:T(1,128)S(1)}, f32[10,1,256]{2,1,0:T(1,128)S(1)}, u32[]{:S(2)}, u32[]{:S(2)}) collective-permute-start(f32[10,1,256]{2,1,0:T(1,128)S(1)} %get-tuple-element.18), channel_id=1, source_target_pairs={{0,1},{1,2},{2,3},{3,4},{4,5},{5,6},{6,7},{8,9},{9,10},{10,11},{11... | collective-permute-start | bytes 30728 | tf_op jit(solution)/shard_map/ppermute | solution.py:36
  73.9 14.9 %collective-permute-start.20 = (f32[1,32,128]{2,1,0:T(8,128)S(1)}, f32[1,32,128]{2,1,0:T(8,128)S(1)}, u32[]{:S(2)}, u32[]{:S(2)}) collective-permute-start(f32[1,32,128]{2,1,0:T(8,128)S(1)} %get-tuple-element.43), channel_id=1, source_target_pairs={{8,0},{16,8},{24,16},{32,24},{40,32},{48,40},{56,48},{64,56},{72,6... | collective-permute-start | bytes 49160 | tf_op jit(solution)/shard_map/ppermute | solution.py:39
  75.2 13.6 %collective-permute-start.21 = (f32[1,32,128]{2,1,0:T(8,128)S(1)}, f32[1,32,128]{2,1,0:T(8,128)S(1)}, u32[]{:S(2)}, u32[]{:S(2)}) collective-permute-start(f32[1,32,128]{2,1,0:T(8,128)S(1)} %get-tuple-element.42), channel_id=1, source_target_pairs={{0,8},{8,16},{16,24},{24,32},{32,40},{40,48},{48,56},{56,64},{64,7... | collective-permute-start | bytes 49160 | tf_op jit(solution)/shard_map/ppermute | solution.py:36
  81.1 23.5 %collective-permute-start.28 = (f32[1,16,64]{2,1,0:T(8,128)S(1)}, f32[1,16,64]{2,1,0:T(8,128)S(1)}, u32[]{:S(2)}, u32[]{:S(2)}) collective-permute-start(f32[1,16,64]{2,1,0:T(8,128)S(1)} %get-tuple-element.57), channel_id=1, source_target_pairs={{8,0},{16,8},{24,16},{32,24},{40,32},{48,40},{56,48},{64,56},{72,6... | collective-permute-start | bytes 12296 | tf_op jit(solution)/shard_map/ppermute | solution.py:39
  82.4 22.2 %collective-permute-start.29 = (f32[1,16,64]{2,1,0:T(8,128)S(1)}, f32[1,16,64]{2,1,0:T(8,128)S(1)}, u32[]{:S(2)}, u32[]{:S(2)}) collective-permute-start(f32[1,16,64]{2,1,0:T(8,128)S(1)} %get-tuple-element.56), channel_id=1, source_target_pairs={{0,8},{8,16},{16,24},{24,32},{32,40},{40,48},{48,56},{56,64},{64,7... | collective-permute-start | bytes 12296 | tf_op jit(solution)/shard_map/ppermute | solution.py:36
  88.8 6.8 %collective-permute-start.22 = (f32[6,1,128]{2,1,0:T(1,128)S(1)}, f32[6,1,128]{2,1,0:T(1,128)S(1)}, u32[]{:S(2)}, u32[]{:S(2)}) collective-permute-start(f32[6,1,128]{2,1,0:T(1,128)S(1)} %get-tuple-element.37), channel_id=1, source_target_pairs={{1,0},{2,1},{3,2},{4,3},{5,4},{6,5},{7,6},{9,8},{10,9},{11,10},{12... | collective-permute-start | bytes 9224 | tf_op jit(solution)/shard_map/ppermute | solution.py:39
  90.7 5.5 %collective-permute-start.23 = (f32[6,1,128]{2,1,0:T(1,128)S(1)}, f32[6,1,128]{2,1,0:T(1,128)S(1)}, u32[]{:S(2)}, u32[]{:S(2)}) collective-permute-start(f32[6,1,128]{2,1,0:T(1,128)S(1)} %get-tuple-element.36), channel_id=1, source_target_pairs={{0,1},{1,2},{2,3},{3,4},{4,5},{5,6},{6,7},{8,9},{9,10},{10,11},{11... | collective-permute-start | bytes 9224 | tf_op jit(solution)/shard_map/ppermute | solution.py:36
  96.5 55.5 %copy-start.4 = (f32[4,32,128]{2,1,0:T(8,128)}, f32[4,32,128]{2,1,0:T(8,128)S(1)}, u32[]{:S(2)}) copy-start(f32[4,32,128]{2,1,0:T(8,128)S(1)} %fusion.243) | copy-start | bytes 196612
  96.6 14.5 %collective-permute-start.24 = (f32[1,32,128]{2,1,0:T(8,128)S(1)}, f32[1,32,128]{2,1,0:T(8,128)S(1)}, u32[]{:S(2)}, u32[]{:S(2)}) collective-permute-start(f32[1,32,128]{2,1,0:T(8,128)S(1)} %get-tuple-element.41), channel_id=1, source_target_pairs={{8,0},{16,8},{24,16},{32,24},{40,32},{48,40},{56,48},{64,56},{72,6... | collective-permute-start | bytes 49160 | tf_op jit(solution)/shard_map/ppermute | solution.py:39
  97.9 13.2 %collective-permute-start.25 = (f32[1,32,128]{2,1,0:T(8,128)S(1)}, f32[1,32,128]{2,1,0:T(8,128)S(1)}, u32[]{:S(2)}, u32[]{:S(2)}) collective-permute-start(f32[1,32,128]{2,1,0:T(8,128)S(1)} %get-tuple-element.40), channel_id=1, source_target_pairs={{0,8},{8,16},{16,24},{24,32},{32,40},{40,48},{48,56},{56,64},{64,7... | collective-permute-start | bytes 49160 | tf_op jit(solution)/shard_map/ppermute | solution.py:36
  104.6 12.0 %collective-permute-start.30 = (f32[4,1,64]{2,1,0:T(1,128)S(1)}, f32[4,1,64]{2,1,0:T(1,128)S(1)}, u32[]{:S(2)}, u32[]{:S(2)}) collective-permute-start(f32[4,1,64]{2,1,0:T(1,128)S(1)} %get-tuple-element.51), channel_id=1, source_target_pairs={{1,0},{2,1},{3,2},{4,3},{5,4},{6,5},{7,6},{9,8},{10,9},{11,10},{12... | collective-permute-start | bytes 3080 | tf_op jit(solution)/shard_map/ppermute | solution.py:39
  106.6 10.1 %collective-permute-start.31 = (f32[4,1,64]{2,1,0:T(1,128)S(1)}, f32[4,1,64]{2,1,0:T(1,128)S(1)}, u32[]{:S(2)}, u32[]{:S(2)}) collective-permute-start(f32[4,1,64]{2,1,0:T(1,128)S(1)} %get-tuple-element.50), channel_id=1, source_target_pairs={{0,1},{1,2},{2,3},{3,4},{4,5},{5,6},{6,7},{8,9},{9,10},{10,11},{11... | collective-permute-start | bytes 3080 | tf_op jit(solution)/shard_map/ppermute | solution.py:36
  111.1 5.7 %collective-permute-start.26 = (f32[6,1,128]{2,1,0:T(1,128)S(1)}, f32[6,1,128]{2,1,0:T(1,128)S(1)}, u32[]{:S(2)}, u32[]{:S(2)}) collective-permute-start(f32[6,1,128]{2,1,0:T(1,128)S(1)} %get-tuple-element.35), channel_id=1, source_target_pairs={{1,0},{2,1},{3,2},{4,3},{5,4},{6,5},{7,6},{9,8},{10,9},{11,10},{12... | collective-permute-start | bytes 9224 | tf_op jit(solution)/shard_map/ppermute | solution.py:39
  113.0 4.4 %collective-permute-start.27 = (f32[6,1,128]{2,1,0:T(1,128)S(1)}, f32[6,1,128]{2,1,0:T(1,128)S(1)}, u32[]{:S(2)}, u32[]{:S(2)}) collective-permute-start(f32[6,1,128]{2,1,0:T(1,128)S(1)} %get-tuple-element.34), channel_id=1, source_target_pairs={{0,1},{1,2},{2,3},{3,4},{4,5},{5,6},{6,7},{8,9},{9,10},{10,11},{11... | collective-permute-start | bytes 9224 | tf_op jit(solution)/shard_map/ppermute | solution.py:36
  118.0 7.7 %collective-permute-start.32 = (f32[1,16,64]{2,1,0:T(8,128)S(1)}, f32[1,16,64]{2,1,0:T(8,128)S(1)}, u32[]{:S(2)}, u32[]{:S(2)}) collective-permute-start(f32[1,16,64]{2,1,0:T(8,128)S(1)} %get-tuple-element.55), channel_id=1, source_target_pairs={{8,0},{16,8},{24,16},{32,24},{40,32},{48,40},{56,48},{64,56},{72,6... | collective-permute-start | bytes 12296 | tf_op jit(solution)/shard_map/ppermute | solution.py:39
  119.3 7.2 %collective-permute-start.33 = (f32[1,16,64]{2,1,0:T(8,128)S(1)}, f32[1,16,64]{2,1,0:T(8,128)S(1)}, u32[]{:S(2)}, u32[]{:S(2)}) collective-permute-start(f32[1,16,64]{2,1,0:T(8,128)S(1)} %get-tuple-element.54), channel_id=1, source_target_pairs={{0,8},{8,16},{16,24},{24,32},{32,40},{40,48},{48,56},{56,64},{64,7... | collective-permute-start | bytes 12296 | tf_op jit(solution)/shard_map/ppermute | solution.py:36
  126.5 25.4 %collective-permute-start.34 = (f32[4,1,64]{2,1,0:T(1,128)S(1)}, f32[4,1,64]{2,1,0:T(1,128)S(1)}, u32[]{:S(2)}, u32[]{:S(2)}) collective-permute-start(f32[4,1,64]{2,1,0:T(1,128)S(1)} %get-tuple-element.49), channel_id=1, source_target_pairs={{1,0},{2,1},{3,2},{4,3},{5,4},{6,5},{7,6},{9,8},{10,9},{11,10},{12... | collective-permute-start | bytes 3080 | tf_op jit(solution)/shard_map/ppermute | solution.py:39
  128.4 23.5 %collective-permute-start.35 = (f32[4,1,64]{2,1,0:T(1,128)S(1)}, f32[4,1,64]{2,1,0:T(1,128)S(1)}, u32[]{:S(2)}, u32[]{:S(2)}) collective-permute-start(f32[4,1,64]{2,1,0:T(1,128)S(1)} %get-tuple-element.48), channel_id=1, source_target_pairs={{0,1},{1,2},{2,3},{3,4},{4,5},{5,6},{6,7},{8,9},{9,10},{10,11},{11... | collective-permute-start | bytes 3080 | tf_op jit(solution)/shard_map/ppermute | solution.py:36
  134.4 30.4 %all-to-all-start = ((f32[128,1,256]{2,1,0:T(1,128)}), f32[128,1,256]{2,1,0:T(1,128)S(1)}, u32[]{:S(2)}, u32[]{:S(2)}) async-start(f32[128,1,256]{2,1,0:T(1,128)} %stack.3), calls=%async_computation | async-start | bytes 262144 | tf_op jit(solution)/shard_map/all_to_all | solution.py:21
  152.1 57.2 %copy-start.5 = (f32[2,16,64]{2,1,0:T(8,128)}, f32[2,16,64]{2,1,0:T(8,128)S(1)}, u32[]{:S(2)}) copy-start(f32[2,16,64]{2,1,0:T(8,128)S(1)} %fusion.296) | copy-start | bytes 24580
  152.1 5.3 %collective-permute-start.36 = (f32[1,16,64]{2,1,0:T(8,128)S(1)}, f32[1,16,64]{2,1,0:T(8,128)S(1)}, u32[]{:S(2)}, u32[]{:S(2)}) collective-permute-start(f32[1,16,64]{2,1,0:T(8,128)S(1)} %get-tuple-element.53), channel_id=1, source_target_pairs={{8,0},{16,8},{24,16},{32,24},{40,32},{48,40},{56,48},{64,56},{72,6... | collective-permute-start | bytes 12296 | tf_op jit(solution)/shard_map/ppermute | solution.py:39
  153.4 4.8 %collective-permute-start.37 = (f32[1,16,64]{2,1,0:T(8,128)S(1)}, f32[1,16,64]{2,1,0:T(8,128)S(1)}, u32[]{:S(2)}, u32[]{:S(2)}) collective-permute-start(f32[1,16,64]{2,1,0:T(8,128)S(1)} %get-tuple-element.52), channel_id=1, source_target_pairs={{0,8},{8,16},{16,24},{24,32},{32,40},{40,48},{48,56},{56,64},{64,7... | collective-permute-start | bytes 12296 | tf_op jit(solution)/shard_map/ppermute | solution.py:36
  158.2 7.1 %collective-permute-start.38 = (f32[4,1,64]{2,1,0:T(1,128)S(1)}, f32[4,1,64]{2,1,0:T(1,128)S(1)}, u32[]{:S(2)}, u32[]{:S(2)}) collective-permute-start(f32[4,1,64]{2,1,0:T(1,128)S(1)} %get-tuple-element.47), channel_id=1, source_target_pairs={{1,0},{2,1},{3,2},{4,3},{5,4},{6,5},{7,6},{9,8},{10,9},{11,10},{12... | collective-permute-start | bytes 3080 | tf_op jit(solution)/shard_map/ppermute | solution.py:39
  162.3 3.2 %collective-permute-start.39 = (f32[4,1,64]{2,1,0:T(1,128)S(1)}, f32[4,1,64]{2,1,0:T(1,128)S(1)}, u32[]{:S(2)}, u32[]{:S(2)}) collective-permute-start(f32[4,1,64]{2,1,0:T(1,128)S(1)} %get-tuple-element.46), channel_id=1, source_target_pairs={{0,1},{1,2},{2,3},{3,4},{4,5},{5,6},{6,7},{8,9},{9,10},{10,11},{11... | collective-permute-start | bytes 3080 | tf_op jit(solution)/shard_map/ppermute | solution.py:36
